TPU v7x, 128 devices: a whole 4x4x4 slice. The times are simulated.
128 devices in a mesh: seq: 16 (over z, y), tp: 8 (over x, core).
Axes of the slice: x: 4, y: 4, z: 4, core: 2. Of those that a mesh axis runs over, the one named last changes fastest.
Arguments:
- hidden: bfloat16 [128, 64, 2560], P(None, 'seq'), may hold values from -6 to 6
- gain_attn: bfloat16 [2560], replicated, may hold values from 0.099609375 to 1.8984375
- w_query: bfloat16 [2560, 2560], P(None, 'tp'), may hold values from -0.125 to 0.125
- w_key: bfloat16 [2560, 640], P(None, 'tp'), may hold values from -0.375 to 0.375
- w_value: bfloat16 [2560, 640], P(None, 'tp'), may hold values from -0.25 to 0.25
- w_out: bfloat16 [2560, 2560], P('tp'), may hold values from -0.125 to 0.125
- gain_ffn: bfloat16 [2560], replicated, may hold values from 0.099609375 to 1.8984375
- w_gate: bfloat16 [2560, 6912], P(None, 'tp'), may hold values from -0.125 to 0.125
- w_up: bfloat16 [2560, 6912], P(None, 'tp'), may hold values from -0.125 to 0.125
- w_down: bfloat16 [6912, 2560], P('tp'), may hold values from -0.078125 to 0.078125
- shared_pages: bfloat16 [320, 8, 2, 80, 128], P('seq', 'tp'), may hold values from -270 to 270
- leaf_pages: bfloat16 [512, 8, 2, 80, 128], P('seq', 'tp'), may hold values from -270 to 270
- root_table: int32 [4, 16], replicated, may hold values from 0 to 319, as said below
- mid_table: int32 [16, 16], replicated, may hold values from 0 to 319, as said below
- leaf_table: int32 [64, 8], replicated, may hold values from 0 to 511, as said below
- root_len: int32 [4], replicated, may hold values from 1024 to 2048, as said below
- mid_len: int32 [16], replicated, may hold values from 1 to 2048, as said below
- leaf_len: int32 [64], replicated, may hold values from 1 to 1024, as said below
- mid_parent: int32 [16], replicated, may hold values from 0 to 3
- leaf_parent: int32 [64], replicated, may hold values from 0 to 15
- slot_request: int32 [64], replicated, may hold values from 0 to 63, as said below
Outputs:
- layer_out: float32 [128, 64, 2560], P('tp', 'seq')
Inputs may be any that keep to these rules, and one draw needn't show every extreme that they name: `slot_request`: A permutation of the requests. The 4 requests of slots 4 * s to 4 * s + 3 have their leaves with 4 distinct owners (see leaf_table). `leaf_table`: all pages of one request's leaf lie with one owner, the index of seq equal to page // 32; each owner holds the leaves of exactly 4 requests, and every leaf page is named once. `root_table`: with mid_table, names every shared page exactly once. Shared page g is held by the index of seq g // 20; each index holds exactly 1 page of every root. `mid_table`: with root_table, names every shared page exactly once. Each index of seq holds exactly 1 page of every middle node. `root_len`: some root reaches the largest value. `mid_len`: some middle node reaches the largest value. `leaf_len`: some leaf reaches the largest value.
All inputs are finite; a program needn't handle non-finite values.
Results may differ from a plain program's by a relative error of at most 0.009.
The roundings to bfloat16 on the way count: a program that leaves them out, or rounds other values in their place, can miss the bound.
Values may be sent and summed in bfloat16 or wider, within the bound.
No kernel may reach another device: no remote copies, remote signals or barrier semaphores. Data moves between devices by JAX's collectives and lax.ppermute only.
A program may use at most 192 MiB of HBM per device.

v0:
```python
import jax
import jax.numpy as jnp
from jax import lax
from jax.sharding import PartitionSpec as P

QH = 32
KVH = 8
HD = 80
WINDOW = 4096
masked_score = -1e30
rope_base = 10000.0


def rms_norm(row_data, gain_vector):
    values = row_data.astype(jnp.float32)
    inverse_rms = lax.rsqrt(jnp.mean(values * values, -1, keepdims=True) + 1e-05)
    return (values * inverse_rms * gain_vector.astype(jnp.float32)).astype(jnp.bfloat16)


def rotate(vector, position):
    half_size = vector.shape[-1] // 2
    frequency = rope_base ** (-2.0 * jnp.arange(half_size, dtype=jnp.float32) / vector.shape[-1])
    angles = position.astype(jnp.float32)[..., None] * frequency
    cos_part = jnp.cos(angles)
    sin_part = jnp.sin(angles)
    first_half = vector[..., :half_size]
    second_half = vector[..., half_size:]
    return jnp.concatenate(
        [
            first_half * cos_part - second_half * sin_part,
            second_half * cos_part + first_half * sin_part,
        ],
        -1,
    )


def page_columns(pages):
    moved = jnp.moveaxis(pages, -5, -2)
    return moved.reshape(moved.shape[:-2] + (moved.shape[-2] * moved.shape[-1],))


def attend(queries, key_pack, key_pos, present, query_pos):
    scores = jnp.einsum(
        "nbkge,bket->nbkgt", queries, key_pack[:, :, 0], preferred_element_type=jnp.float32
    ) * queries.shape[-1] ** (-0.5)
    distance = query_pos[:, :, None] - key_pos[None, :, :]
    allowed = (present[None, :, :] & (distance >= 0) & (distance < WINDOW))[:, :, None, None, :]
    scores = jnp.where(allowed, scores, masked_score)
    maximum = jnp.max(scores, -1)
    weights = jnp.where(allowed, jnp.exp(scores - maximum[..., None]), 0.0)
    totals = jnp.sum(weights, -1)
    weighted = jnp.einsum(
        "nbkgt,bket->nbkge",
        weights.astype(jnp.bfloat16),
        key_pack[:, :, 1],
        preferred_element_type=jnp.float32,
    )
    return (weighted, maximum, totals)


def merge_parts(first, second):
    maximum = jnp.maximum(first[1], second[1])
    first_scale = jnp.exp(first[1] - maximum)
    second_scale = jnp.exp(second[1] - maximum)
    return (
        first[0] * first_scale[..., None] + second[0] * second_scale[..., None],
        maximum,
        first[2] * first_scale + second[2] * second_scale,
    )


def spans(request_ids, root_len, mid_len, leaf_len, mid_parent, leaf_parent):
    mid_nodes = leaf_parent[request_ids]
    root_nodes = mid_parent[mid_nodes]
    return (root_nodes, mid_nodes, root_len[root_nodes], mid_len[mid_nodes], leaf_len[request_ids])


def shards(
    hidden,
    gain_attn,
    w_query,
    w_key,
    w_value,
    w_out,
    gain_ffn,
    w_gate,
    w_up,
    w_down,
    shared_pages,
    leaf_pages,
    root_table,
    mid_table,
    leaf_table,
    root_len,
    mid_len,
    leaf_len,
    mid_parent,
    leaf_parent,
    slot_request,
):
    new_rows, local_reqs, model_width = hidden.shape
    seq_count = lax.axis_size("seq")
    seq_index = lax.axis_index("seq")
    kv_local = leaf_pages.shape[1]
    group_size = QH // KVH
    pages_here = leaf_pages.shape[0]
    slot_ids = seq_index * local_reqs + jnp.arange(local_reqs, dtype=jnp.int32)
    requests = slot_request[slot_ids]
    root_nodes, mid_nodes, root_span, mid_span, leaf_span = spans(
        requests, root_len, mid_len, leaf_len, mid_parent, leaf_parent
    )
    context = root_span + mid_span + leaf_span
    new_index = jnp.arange(new_rows, dtype=jnp.int32)
    query_pos = context[None, :] + new_index[:, None]
    all_slots = slot_request.reshape(seq_count, local_reqs)
    page_store = lax.all_gather(shared_pages, "seq", axis=0, tiled=True)
    root_index = root_table[root_nodes]
    mid_index = mid_table[mid_nodes]
    normed = rms_norm(hidden, gain_attn).reshape(-1, model_width)
    query_proj = jnp.dot(normed, w_query, preferred_element_type=jnp.float32).reshape(
        new_rows, local_reqs, -1, HD
    )
    queries = (
        rotate(query_proj, query_pos[:, :, None])
        .astype(jnp.bfloat16)
        .reshape(new_rows, local_reqs, kv_local, group_size, HD)
    )
    key_proj = jnp.dot(normed, w_key, preferred_element_type=jnp.float32).reshape(
        new_rows, local_reqs, kv_local, HD
    )
    new_keys = rotate(key_proj, query_pos[:, :, None]).astype(jnp.bfloat16)
    new_values = (
        jnp.dot(normed, w_value, preferred_element_type=jnp.float32)
        .astype(jnp.bfloat16)
        .reshape(new_rows, local_reqs, kv_local, HD)
    )
    home_of = leaf_table[:, 0] // pages_here
    own_homes = home_of[requests]
    sender_match = home_of[all_slots] == seq_index
    sender_pick = jnp.argmax(sender_match, 1)
    sender_have = jnp.any(sender_match, 1)
    picked_request = jnp.take_along_axis(all_slots, sender_pick[:, None], 1)[:, 0]
    page_ids = jnp.where(
        sender_have[:, None], leaf_table[picked_request] - seq_index * pages_here, 0
    )
    leaf_steps = jnp.arange(leaf_table.shape[1] * leaf_pages.shape[-1], dtype=jnp.int32)
    fresh_pack = jnp.stack(
        [jnp.transpose(new_keys, (1, 2, 3, 0)), jnp.transpose(new_values, (1, 2, 3, 0))], 2
    )
    fresh_part = attend(
        queries,
        fresh_pack,
        context[:, None] + new_index[None, :],
        jnp.ones((local_reqs, new_rows), bool),
        query_pos,
    )
    outgoing = jnp.where(
        sender_have[:, None, None, None, None, None], jnp.take(leaf_pages, page_ids, axis=0), 0
    )
    arrived = lax.all_to_all(outgoing, "seq", split_axis=0, concat_axis=0, tiled=True)
    leaf_pack = page_columns(jnp.take(arrived, own_homes, axis=0))
    leaf_pos = (root_span + mid_span)[:, None] + leaf_steps[None, :]
    leaf_part = attend(
        queries, leaf_pack, leaf_pos, leaf_steps[None, :] < leaf_span[:, None], query_pos
    )
    root_pack = page_columns(jnp.take(page_store, root_index, axis=0))
    root_steps = jnp.arange(root_pack.shape[-1], dtype=jnp.int32)
    root_part = attend(
        queries,
        root_pack,
        root_steps[None, :] + 0 * root_span[:, None],
        root_steps[None, :] < root_span[:, None],
        query_pos,
    )
    mid_pack = page_columns(jnp.take(page_store, mid_index, axis=0))
    mid_steps = jnp.arange(mid_pack.shape[-1], dtype=jnp.int32)
    mid_part = attend(
        queries,
        mid_pack,
        root_span[:, None] + mid_steps[None, :],
        mid_steps[None, :] < mid_span[:, None],
        query_pos,
    )
    combined = merge_parts(merge_parts(root_part, mid_part), merge_parts(leaf_part, fresh_part))
    attended = (
        (combined[0] / combined[2][..., None])
        .astype(jnp.bfloat16)
        .reshape(new_rows * local_reqs, -1)
    )
    attn_proj = lax.psum(jnp.dot(attended, w_out, preferred_element_type=jnp.float32), "tp")
    resid = hidden.astype(jnp.float32) + attn_proj.reshape(new_rows, local_reqs, model_width)
    normed_ffn = rms_norm(resid, gain_ffn).reshape(-1, model_width)
    gate_rows = jnp.dot(normed_ffn, w_gate, preferred_element_type=jnp.float32)
    up_rows = jnp.dot(normed_ffn, w_up, preferred_element_type=jnp.float32)
    activated = (
        (jax.nn.silu(gate_rows) * up_rows).astype(jnp.bfloat16).reshape(new_rows, local_reqs, -1)
    )
    own_count = new_rows // lax.axis_size("tp")
    ffn_proj = lax.psum_scatter(
        jnp.dot(
            activated.reshape(-1, activated.shape[-1]), w_down, preferred_element_type=jnp.float32
        ).reshape(own_count * lax.axis_size("tp"), local_reqs, model_width),
        "tp",
        scatter_dimension=0,
        tiled=True,
    )
    own_rows = lax.dynamic_slice_in_dim(resid, lax.axis_index("tp") * own_count, own_count, 0)
    return own_rows + ffn_proj


def solution(mesh):
    return jax.shard_map(
        shards,
        mesh=mesh,
        in_specs=(
            P(None, "seq", None),
            P(),
            P(None, "tp"),
            P(None, "tp"),
            P(None, "tp"),
            P("tp", None),
            P(),
            P(None, "tp"),
            P(None, "tp"),
            P("tp", None),
            P("seq", "tp", None, None, None),
            P("seq", "tp", None, None, None),
            P(),
            P(),
            P(),
            P(),
            P(),
            P(),
            P(),
            P(),
            P(),
        ),
        out_specs=P("tp", "seq", None),
        check_vma=False,
    )
```

profile of v0, /device:TPU:1, one launch (start us, length us, event | category | flops | bytes accessed | tf_op | source)
XLA Modules:
  0.0 451.2 jit_solution(16612270365806220123)
XLA Ops:
  8.8 0.8 copy.88
  10.3 0.8 gather_fusion.9
  13.6 3.6 gather_fusion.11
  17.2 5.5 %select_select_fusion = bf16[16,8,1,2,80,128]{5,4,3,1,2,0:T(8,128)(2,1)} fusion(bf16[16,8,1,2,80,128]{5,4,3,1,2,0:T(8,128)(2,1)} %bitcast.320, pred[16]{0:T(512)(128)(4,1)S(1)} %reduce_or.9, pred[16,8]{1,0:T(8,128)(4,1)S(1)} %get-tuple-element.17), kind=kLoop, calls=%fused_computation.47 | loop fusion | flops 5242880 | bytes 10485904 | tf_op jit(solution)/shard_map/jit(_where)/select_n | solution.py:157
  22.7 8.8 %all-to-all-start = ((bf16[16,8,1,2,80,128]{5,4,3,1,2,0:T(8,128)(2,1)}), bf16[16,8,1,2,80,128]{5,4,3,1,2,0:T(8,128)(2,1)}, u32[]{:S(2)}, u32[]{:S(2)}) async-start(bf16[16,8,1,2,80,128]{5,4,3,1,2,0:T(8,128)(2,1)} %select_select_fusion), calls=%async_computation | async-start | bytes 10485760 | tf_op jit(solution)/shard_map/all_to_all | solution.py:160
  37.5 3.4 fusion.17
  40.9 3.0 fusion.19
  44.0 5.8 %reshape.793 = bf16[512,2560]{1,0:T(8,128)(2,1)} reshape(bf16[128,4,2560]{2,1,0:T(4,128)(2,1)} %fusion.19) | data formatting | bytes 5242880 | tf_op jit(solution)/shard_map/reshape | solution.py:119
  49.8 2.6 convolution_convert_fusion
  52.4 0.8 copy.94
  55.5 2.8 fusion.73
  58.4 1.5 fusion.135
  60.4 1.1 fusion.30
  64.8 1.4 fusion.37
  66.5 5.5 %fusion.26 = (pred[128,4,2048]{0,2,1:T(8,128)(4,1)}, pred[128,4,2048]{0,2,1:T(8,128)(4,1)}) fusion(s32[128,4]{0,1:T(4,128)S(1)} %get-tuple-element.29, pred[4,2048]{1,0:T(4,128)(4,1)S(1)} %iota_compare_fusion.1, s32[4,2048]{1,0:T(4,128)S(1)} %iota_add_fusion, pred[4,2048]{1,0:T(4,128)(4,1)S(1)} %iota_compare_fusion), kind=kLoop, calls=%fused_computation.54 | loop fusion | flops 10485760 | bytes 2148352 | tf_op jit(solution)/shard_map/and | solution.py:47
  72.0 55.6 %all-to-all-done = bf16[16,8,1,2,80,128]{5,4,3,1,2,0:T(8,128)(2,1)} async-done(((bf16[16,8,1,2,80,128]{5,4,3,1,2,0:T(8,128)(2,1)}), bf16[16,8,1,2,80,128]{5,4,3,1,2,0:T(8,128)(2,1)}, u32[]{:S(2)}, u32[]{:S(2)}) %all-to-all-start) | async-done | bytes 5242912 | tf_op jit(solution)/shard_map/all_to_all | solution.py:160
  127.6 3.4 gather_fusion.12
  131.0 0.8 fusion.41
  132.3 1.5 reshape.788
  133.8 2.5 fusion.14
  136.3 3.2 copy-done.11
  139.7 2.7 fusion.15
  142.3 16.8 %all-gather.2.cloned.1.call-done = bf16[320,1,2,80,128]{4,3,2,1,0:T(8,128)(2,1)} async-done(((bf16[20,1,2,80,128]{4,3,2,1,0:T(8,128)(2,1)}), bf16[320,1,2,80,128]{4,3,2,1,0:T(8,128)(2,1)}) %all-gather.2.cloned.1.call-update) | async-done | bytes 13107216 | tf_op jit(solution)/shard_map/all_gather | solution.py:116
  159.2 7.1 %gather_fusion.15 = bf16[64,2,80,128]{3,2,1,0:T(8,128)(2,1)} fusion(bf16[320,2,80,128]{3,2,1,0:T(8,128)(2,1)} %bitcast.326, s32[1024]{0:T(1024)S(1)} %copy-done.31), kind=kCustom, calls=%fused_computation.1.clone | custom fusion | bytes 5243136 | tf_op jit(solution)/shard_map/jit(_take)/gather | solution.py:175
  166.2 7.2 %gather_fusion.14 = bf16[64,2,80,128]{3,2,1,0:T(8,128)(2,1)} fusion(bf16[320,2,80,128]{3,2,1,0:T(8,128)(2,1)} %bitcast.327, s32[1024]{0:T(1024)S(1)} %copy-done.30), kind=kCustom, calls=%fused_computation.clone | custom fusion | bytes 5243136 | tf_op jit(solution)/shard_map/jit(_take)/gather | solution.py:166
  173.4 4.2 fusion.35
  177.6 5.2 %reshape.777 = bf16[4,1,2,80,2048]{4,3,0,2,1:T(8,128)(2,1)} reshape(bf16[4,1,2,80,16,128]{5,4,3,0,2,1:T(8,128)(2,1)} %fusion.35) | data formatting | bytes 5242880 | tf_op jit(solution)/shard_map/reshape | solution.py:39
  182.8 4.3 fusion.34
  187.1 5.2 %reshape.781 = bf16[4,1,2,80,2048]{4,3,0,2,1:T(8,128)(2,1)} reshape(bf16[4,1,2,80,16,128]{5,4,3,0,2,1:T(8,128)(2,1)} %fusion.34) | data formatting | bytes 5242880 | tf_op jit(solution)/shard_map/reshape | solution.py:39
  192.3 8.8 %fusion.1 = (f32[128,4,4]{0,2,1:T(4,128)S(1)}, f32[4,2048,128,4]{2,1,3,0:T(8,128)}) fusion(pred[128,4,2048]{0,2,1:T(8,128)(4,1)S(1)} %copy-done.13, bf16[128,4,4,40]{0,3,2,1:T(8,128)(2,1)S(1)} %copy-done.24, bf16[128,4,4,40]{0,3,2,1:T(8,128)(2,1)S(1)} %copy-done.22, bf16[4,1,2,80,2048]{4,3,0,2,1:T(8,128)(2,1)} %reshape.781), kind=kOutput, calls=%fused_computation.21 | convolution fusion | flops 684324864 | bytes 19472384 | tf_op jit(solution)/shard_map/nbkge,bket->nbkgt/dot_general | solution.py:43
  201.1 2.7 fusion
  203.9 10.7 %fusion.2 = (f32[128,4,4]{0,2,1:T(4,128)S(1)}, f32[128,4,4]{0,2,1:T(4,128)S(1)}) fusion(f32[4,2048,128,4]{2,1,3,0:T(8,128)S(1)} %get-tuple-element.38, f32[128,4,4]{0,2,1:T(4,128)S(1)} %get-tuple-element.37, pred[128,4,2048]{0,2,1:T(8,128)(4,1)S(1)} %copy-done.12, f32[128,4,4]{0,2,1:T(4,128)S(1)} %get-tuple-element.31, ...), kind=kLoop, calls=%fused_computation.22 | loop fusion | flops 41938944 | bytes 35684352 | tf_op jit(solution)/shard_map/reduce_sum | solution.py:51
  214.7 3.0 fusion.56
  217.7 10.7 %fusion.68 = f32[128,4,1,4,80]{0,4,3,1,2:T(8,128)} fusion(f32[4,2048,128,4]{2,1,3,0:T(8,128)} %get-tuple-element.32, f32[128,4,4]{0,2,1:T(4,128)S(1)} %get-tuple-element.31, pred[128,4,2048]{0,2,1:T(8,128)(4,1)S(1)} %copy-done.13, bf16[4,1,2,80,2048]{4,3,0,2,1:T(8,128)(2,1)} %reshape.781, f32[128,4,4]{0,2,1:T(4,128)S(1)} %bitcast.342), kind=kOutput, calls=%fused_computation.94 | convolution fusion | flops 692224000 | bytes 19808256 | tf_op jit(solution)/shard_map/nbkgt,bket->nbkge/dot_general | solution.py:52
  228.4 5.8 %fusion.65 = f32[128,4,1,4,80]{0,4,3,1,2:T(8,128)} fusion(f32[128,4,1,4,80]{0,4,3,1,2:T(8,128)} %fusion.68, f32[4,2048,128,4]{2,1,3,0:T(8,128)S(1)} %get-tuple-element.38, f32[128,4,4]{0,2,1:T(4,128)S(1)} %get-tuple-element.37, pred[128,4,2048]{0,2,1:T(8,128)(4,1)S(1)} %copy-done.12, bf16[4,1,2,80,2048]{4,3,0,2,1:T(8,128)(2,1)} %reshape.777, ...), kind=kOutput, calls=%fused_computation.93 | convolution fusion | flops 692551680 | bytes 20471808 | tf_op jit(solution)/shard_map/nbkgt,bket->nbkge/dot_general | solution.py:52
  234.2 1.7 fusion.72
  236.7 3.9 fusion.123
  240.6 7.1 %reshape.798 = f32[128,4,2560]{2,1,0:T(4,128)} reshape(f32[512,2560]{1,0:T(8,128)} %fusion.123) | data formatting | bytes 10485760 | tf_op jit(solution)/shard_map/reshape | solution.py:191
  248.4 76.4 %all-reduce.4.cloned.1.call-done = f32[128,4,2560]{2,1,0:T(4,128)} async-done(((f32[128,4,2560]{2,1,0:T(4,128)}), f32[128,4,2560]{2,1,0:T(4,128)}) %all-reduce.4.cloned.1.call-update) | async-done | bytes 5242896 | tf_op jit(solution)/shard_map/psum | solution.py:190
  324.8 5.1 %multiply_reduce_fusion = (f32[128,4]{1,0:T(8,128)S(1)}, f32[128,4,2560]{2,1,0:T(4,128)S(1)}) fusion(f32[128,4,2560]{2,1,0:T(4,128)} %all-reduce.4.cloned.1.call-done, bf16[128,4,2560]{2,1,0:T(4,128)(2,1)} %param.23), kind=kLoop, calls=%fused_computation.46 | loop fusion | flops 5242368 | bytes 13109248 | tf_op jit(solution)/shard_map/reduce_sum | solution.py:16
  329.9 2.3 copy-done.9
  332.2 2.7 multiply_convert_fusion
  334.9 5.6 %reshape.799 = bf16[512,2560]{1,0:T(8,128)(2,1)} reshape(bf16[128,4,2560]{2,1,0:T(4,128)(2,1)} %multiply_convert_fusion) | data formatting | bytes 5242880 | tf_op jit(solution)/shard_map/reshape | solution.py:192
  340.5 5.5 %fusion.124 = f32[512,864]{0,1:T(8,128)S(1)} fusion(bf16[512,2560]{1,0:T(8,128)(2,1)} %reshape.799, bf16[2560,864]{0,1:T(8,128)(2,1)} %param.30), kind=kOutput, calls=%fused_computation.214 | convolution fusion | flops 2264924160 | bytes 8814592 | tf_op jit(solution)/shard_map/dot_general | solution.py:193
  346.0 12.0 %fusion.78 = f32[512,2560]{1,0:T(8,128)} fusion(bf16[864,2560]{1,0:T(8,128)(2,1)} %param.32, f32[512,864]{0,1:T(8,128)S(1)} %fusion.124, bf16[512,2560]{1,0:T(8,128)(2,1)} %reshape.799, bf16[2560,864]{0,1:T(8,128)(2,1)} %param.31), kind=kOutput, calls=%fused_computation.102 | convolution fusion | flops 4532502528 | bytes 18481152 | tf_op jit(solution)/shard_map/dot_general | solution.py:200
  358.1 7.1 %reshape.800 = f32[128,4,2560]{2,1,0:T(4,128)} reshape(f32[512,2560]{1,0:T(8,128)} %fusion.78) | data formatting | bytes 10485760 | tf_op jit(solution)/shard_map/reshape | solution.py:202
  367.1 75.0 %all-reduce.6.cloned.1.call-done = f32[128,4,2560]{2,1,0:T(4,128)} async-done(((f32[128,4,2560]{2,1,0:T(4,128)}), f32[128,4,2560]{2,1,0:T(4,128)}) %all-reduce.6.cloned.1.call-update) | async-done | bytes 5242896
  442.1 2.3 dynamic-slice_add_fusion
  (163 shorter events, 21.2 us)
Async XLA Ops:
  6.5 230.2 %copy-start = (bf16[320,2560]{1,0:T(8,128)(2,1)S(1)}, bf16[320,2560]{1,0:T(8,128)(2,1)}, u32[]{:S(2)}) copy-start(bf16[320,2560]{1,0:T(8,128)(2,1)} %param.28) | copy-start | bytes 4915204
  6.5 152.6 %all-gather.2.cloned.1.call-start = ((), (), s32[]{:S(2)}) async-start(), calls=%async_computation.1 | async-start | bytes 13926400 | tf_op jit(solution)/shard_map/all_gather | solution.py:116
  10.3 3.3 copy-start.10
  22.7 9.0 %copy-start.1 = (s32[64]{0:T(128)S(1)}, s32[64]{0:T(128)}, u32[]{:S(2)}) copy-start(s32[64]{0:T(128)} %param.43) | copy-start | bytes 772
  22.7 10.3 %copy-start.2 = (s32[64]{0:T(128)S(1)}, s32[64]{0:T(128)}, u32[]{:S(2)}) copy-start(s32[64]{0:T(128)} %param.40) | copy-start | bytes 772
  22.7 10.9 %copy-start.3 = (s32[64]{0:T(128)S(1)}, s32[64]{0:T(128)}, u32[]{:S(2)}) copy-start(s32[64]{0:T(128)} %param.42) | copy-start | bytes 772
  22.7 11.6 %copy-start.4 = (s32[16]{0:T(128)S(1)}, s32[16]{0:T(128)}, u32[]{:S(2)}) copy-start(s32[16]{0:T(128)} %param.39) | copy-start | bytes 196
  22.7 12.2 %copy-start.5 = (s32[16]{0:T(128)S(1)}, s32[16]{0:T(128)}, u32[]{:S(2)}) copy-start(s32[16]{0:T(128)} %param.41) | copy-start | bytes 196
  22.7 12.9 %copy-start.26 = (s32[16,16]{1,0:T(8,128)S(1)}, s32[16,16]{1,0:T(8,128)}, u32[]{:S(2)}) copy-start(s32[16,16]{1,0:T(8,128)} %param.36) | copy-start | bytes 3076
  22.7 13.5 %copy-start.6 = (s32[4]{0:T(128)S(1)}, s32[4]{0:T(128)}, u32[]{:S(2)}) copy-start(s32[4]{0:T(128)} %param.38) | copy-start | bytes 52
  22.7 14.2 %copy-start.25 = (s32[4,16]{1,0:T(4,128)S(1)}, s32[4,16]{1,0:T(4,128)}, u32[]{:S(2)}) copy-start(s32[4,16]{1,0:T(4,128)} %param.35) | copy-start | bytes 772
  22.7 14.8 %copy-start.32 = (bf16[2560]{0:T(1024)(128)(2,1)S(1)}, bf16[2560]{0:T(1024)(128)(2,1)}, u32[]{:S(2)}) copy-start(bf16[2560]{0:T(1024)(128)(2,1)} %param.24) | copy-start | bytes 15364
  22.7 104.8 %all-to-all-start = ((bf16[16,8,1,2,80,128]{5,4,3,1,2,0:T(8,128)(2,1)}), bf16[16,8,1,2,80,128]{5,4,3,1,2,0:T(8,128)(2,1)}, u32[]{:S(2)}, u32[]{:S(2)}) async-start(bf16[16,8,1,2,80,128]{5,4,3,1,2,0:T(8,128)(2,1)} %select_select_fusion), calls=%async_computation | async-start | bytes 10485760 | tf_op jit(solution)/shard_map/all_to_all | solution.py:160
  31.6 293.2 %all-reduce.4.cloned.1.call-start = ((), (), s32[]{:S(2)}) async-start(), calls=%async_computation.2 | async-start | bytes 10485760 | tf_op jit(solution)/shard_map/psum | solution.py:190
  37.5 3.4 copy-start.7
  40.9 8.9 %copy-start.20 = (bf16[2560,80]{0,1:T(8,128)(2,1)S(1)}, bf16[2560,80]{0,1:T(8,128)(2,1)}, u32[]{:S(2)}) copy-start(bf16[2560,80]{0,1:T(8,128)(2,1)} %param.27) | copy-start | bytes 1228804
  44.0 11.6 %copy-start.37 = (bf16[2560,80]{0,1:T(8,128)(2,1)S(1)}, bf16[2560,80]{0,1:T(8,128)(2,1)}, u32[]{:S(2)}) copy-start(bf16[2560,80]{0,1:T(8,128)(2,1)} %param.26) | copy-start | bytes 1228804
  53.2 5.2 %copy-start.8 = (bf16[128,4,2560]{2,1,0:T(4,128)(2,1)S(1)}, bf16[128,4,2560]{2,1,0:T(4,128)(2,1)}, u32[]{:S(2)}) copy-start(bf16[128,4,2560]{2,1,0:T(4,128)(2,1)} %param.23) | copy-start | bytes 7864324
  55.5 4.9 %copy-start.36 = (bf16[2560,320]{0,1:T(8,128)(2,1)S(1)}, bf16[2560,320]{0,1:T(8,128)(2,1)}, u32[]{:S(2)}) copy-start(bf16[2560,320]{0,1:T(8,128)(2,1)} %param.25) | copy-start | bytes 4915204
  61.6 0.7 copy-start.21
  61.6 1.0 copy-start.23
  62.7 2.1 copy-start.18
  66.2 70.1 %copy-start.15 = (pred[128,4,1024]{0,2,1:T(8,128)(4,1)}, pred[128,4,1024]{0,2,1:T(8,128)(4,1)S(1)}, u32[]{:S(2)}) copy-start(pred[128,4,1024]{0,2,1:T(8,128)(4,1)S(1)} %fusion.37) | copy-start | bytes 1572868
  136.3 3.2 copy-start.11
  136.3 3.3 copy-start.27
  139.7 19.5 %copy-start.31 = (s32[1024]{0:T(1024)S(1)}, s32[1024]{0:T(1024)}, u32[]{:S(2)}) copy-start(s32[1024]{0:T(1024)} %pad_clamp_fusion.4) | copy-start | bytes 12292
  142.3 23.9 %copy-start.30 = (s32[1024]{0:T(1024)S(1)}, s32[1024]{0:T(1024)}, u32[]{:S(2)}) copy-start(s32[1024]{0:T(1024)} %pad_clamp_fusion.5) | copy-start | bytes 12292
  159.2 14.3 %copy-start.35 = (pred[4,16]{1,0:T(4,128)(4,1)S(1)}, pred[4,16]{1,0:T(4,128)(4,1)}, u32[]{:S(2)}) copy-start(pred[4,16]{1,0:T(4,128)(4,1)} %compare_and_fusion.2) | copy-start | bytes 196
  173.4 9.4 %copy-start.34 = (pred[4,16]{1,0:T(4,128)(4,1)S(1)}, pred[4,16]{1,0:T(4,128)(4,1)}, u32[]{:S(2)}) copy-start(pred[4,16]{1,0:T(4,128)(4,1)} %compare_and_fusion.1) | copy-start | bytes 196
  182.8 9.5 %copy-start.13 = (pred[128,4,2048]{0,2,1:T(8,128)(4,1)S(1)}, pred[128,4,2048]{0,2,1:T(8,128)(4,1)}, u32[]{:S(2)}) copy-start(pred[128,4,2048]{0,2,1:T(8,128)(4,1)} %get-tuple-element.28) | copy-start | bytes 3145732
  182.8 9.5 %copy-start.22 = (bf16[128,4,4,40]{0,3,2,1:T(8,128)(2,1)S(1)}, bf16[128,4,4,40]{0,3,2,1:T(8,128)(2,1)}, u32[]{:S(2)}) copy-start(bf16[128,4,4,40]{0,3,2,1:T(8,128)(2,1)} %copy-done.21) | copy-start | bytes 491524
  182.8 9.5 %copy-start.24 = (bf16[128,4,4,40]{0,3,2,1:T(8,128)(2,1)S(1)}, bf16[128,4,4,40]{0,3,2,1:T(8,128)(2,1)}, u32[]{:S(2)}) copy-start(bf16[128,4,4,40]{0,3,2,1:T(8,128)(2,1)} %copy-done.23) | copy-start | bytes 491524
  192.3 8.8 %copy-start.12 = (pred[128,4,2048]{0,2,1:T(8,128)(4,1)S(1)}, pred[128,4,2048]{0,2,1:T(8,128)(4,1)}, u32[]{:S(2)}) copy-start(pred[128,4,2048]{0,2,1:T(8,128)(4,1)} %get-tuple-element.27) | copy-start | bytes 3145732
  192.3 8.8 %copy-start.14 = (bf16[4,1,2,80,2048]{4,3,0,2,1:T(8,128)(2,1)S(1)}, bf16[4,1,2,80,2048]{4,3,0,2,1:T(8,128)(2,1)}, u32[]{:S(2)}) copy-start(bf16[4,1,2,80,2048]{4,3,0,2,1:T(8,128)(2,1)} %reshape.777) | copy-start | bytes 7864324
  201.1 13.6 %slice-start = ((s8[8388608]{0:T(1024)(128)(4,1)}), s8[4194304]{0:T(1024)(128)(4,1)S(1)}, s32[]{:S(2)}) async-start(s8[8388608]{0:T(1024)(128)(4,1)} %bitcast.324), calls=%async_computation.4 | async-start | bytes 8388608
  203.9 10.8 %copy-start.28 = (f32[128,4,4]{0,2,1:T(4,128)S(1)}, f32[128,4,4]{0,2,1:T(4,128)}, u32[]{:S(2)}) copy-start(f32[128,4,4]{0,2,1:T(4,128)} %copy-done.27) | copy-start | bytes 24580
  203.9 10.8 %copy-start.29 = (f32[128,4,4]{0,2,1:T(4,128)S(1)}, f32[128,4,4]{0,2,1:T(4,128)}, u32[]{:S(2)}) copy-start(f32[128,4,4]{0,2,1:T(4,128)} %fusion.15) | copy-start | bytes 24580
  203.9 10.8 %slice-start.1 = ((s8[8388608]{0:T(1024)(128)(4,1)}), s8[4194304]{0:T(1024)(128)(4,1)S(1)}, s32[]{:S(2)}) async-start(s8[8388608]{0:T(1024)(128)(4,1)} %bitcast.324), calls=%async_computation.5 | async-start | bytes 8388608
  203.9 10.8 %copy-start.16 = (pred[128,4,1024]{0,2,1:T(8,128)(4,1)S(1)}, pred[128,4,1024]{0,2,1:T(8,128)(4,1)}, u32[]{:S(2)}) copy-start(pred[128,4,1024]{0,2,1:T(8,128)(4,1)} %copy-done.15) | copy-start | bytes 1572868
  203.9 10.8 %copy-start.17 = (bf16[4,1,2,80,1024]{4,3,0,2,1:T(8,128)(2,1)S(1)}, bf16[4,1,2,80,1024]{4,3,0,2,1:T(8,128)(2,1)}, u32[]{:S(2)}) copy-start(bf16[4,1,2,80,1024]{4,3,0,2,1:T(8,128)(2,1)} %reshape.788) | copy-start | bytes 3932164
  228.4 5.8 %copy-start.19 = (f32[128,4,1,4,128]{0,4,3,1,2:T(8,128)S(1)}, f32[128,4,1,4,128]{0,4,3,1,2:T(8,128)}, u32[]{:S(2)}) copy-start(f32[128,4,1,4,128]{0,4,3,1,2:T(8,128)} %copy-done.18) | copy-start | bytes 3145732
  247.7 0.7 copy-start.33
  247.7 194.3 %all-reduce.6.cloned.1.call-start = ((), (), s32[]{:S(2)}) async-start(), calls=%async_computation.3 | async-start | bytes 10485760
  329.9 2.3 copy-start.9
  365.2 0.7 copy-start.38
Sparse Core Ops, SparseCore 0:
  9.5 149.6 all-gather.1
  247.8 76.8 all-reduce.3
  365.3 76.6 all-reduce.5
where the time goes:
time: 457 us; the launch traced here: 451 us
  waiting for transfers between devices  225 us (49%)
  local copies, waits for them, and re-layouts  79.4 us (17%)
  matrix products  63.6 us (14%)
  other arithmetic  60 us (13%)
  between operations  14.6 us (3%)
  starting transfers between devices  8.91 us (2%)
    psum x1, waiting for transfers between devices, shards(): lax.psum(jnp.dot(attended, w_out, preferred_element_type=jnp.float32), 'tp')  76.4 us
    unnamed x4, waiting for transfers between devices  75.7 us
    all_to_all x1, waiting for transfers between devices, shards(): lax.all_to_all(outgoing, 'seq', split_axis=0, concat_axis=0, tiled=True)  55.6 us
    dot_general x4, matrix products, attend(): jnp.einsum('nbkgt,bket->nbkge', weights.astype(jnp.bfloat16), key_pack[:,...  21.1 us
    all_gather x1, waiting for transfers between devices, shards(): page_store = lax.all_gather(shared_pages, 'seq', axis=0, tiled=True)  16.8 us
    dot_general x4, matrix products, attend(): jnp.einsum('nbkge,bket->nbkgt', queries, key_pack[:, :, 0], preferred_ele...  14.5 us
    reduce_sum x3, other arithmetic, attend(): totals = jnp.sum(weights, -1)  13.6 us
    dot_general x1, matrix products, shards(): jnp.dot(activated.reshape(-1, activated.shape[-1]), w_down, preferred_ele...  12 us
  transfers between devices with their start and end apart: 4, of which 4 were waited for; matrix products, arithmetic and copies ran while one was open for 15% of the time, Pallas kernels for 0%

commit v1 on v0

--- a/solution.py
+++ b/solution.py
@@ -187,7 +187,9 @@
         .astype(jnp.bfloat16)
         .reshape(new_rows * local_reqs, -1)
     )
-    attn_proj = lax.psum(jnp.dot(attended, w_out, preferred_element_type=jnp.float32), "tp")
+    x = jnp.dot(attended, w_out, preferred_element_type=jnp.float32)
+    terms = lax.all_gather(x, "tp")
+    attn_proj = jnp.sum(terms, axis=0)
     resid = hidden.astype(jnp.float32) + attn_proj.reshape(new_rows, local_reqs, model_width)
     normed_ffn = rms_norm(resid, gain_ffn).reshape(-1, model_width)
     gate_rows = jnp.dot(normed_ffn, w_gate, preferred_element_type=jnp.float32)

time: 457 us -> 591 us (1.29)
  waiting for transfers between devices: 225 us -> 340 us
  other arithmetic: 60 us -> 78.9 us
    all_gather x0 -> x1, waiting for transfers between devices: none -> 193 us  [shards(): terms = lax.all_gather(x, 'tp')]
    psum x1 -> x0, waiting for transfers between devices: 76.4 us -> none  [shards(): lax.psum(jnp.dot(attended, w_out, preferred_element_type=jnp.float32), 'tp')]
    reduce_sum x0 -> x1, other arithmetic: none -> 18.9 us  [shards(): attn_proj = jnp.sum(terms, axis=0)]
  transfers between devices with their start and end apart: 4 -> 4, of which waited for: 4 -> 4; matrix products, arithmetic and copies ran while one was open for 15% -> 11% of each run, Pallas kernels for 0% -> 0%
where the time goes in v1:
time: 591 us; the launch traced here: 585 us
  waiting for transfers between devices  340 us (58%)
  local copies, waits for them, and re-layouts  79.1 us (13%)
  other arithmetic  78.9 us (13%)
  matrix products  63.6 us (11%)
  between operations  14.6 us (2%)
  starting transfers between devices  8.91 us (2%)
    all_gather x1, waiting for transfers between devices, shards(): terms = lax.all_gather(x, 'tp')  193 us
    unnamed x4, waiting for transfers between devices  74.1 us
    all_to_all x1, waiting for transfers between devices, shards(): lax.all_to_all(outgoing, 'seq', split_axis=0, concat_axis=0, tiled=True)  55.7 us
    dot_general x4, matrix products, attend(): jnp.einsum('nbkgt,bket->nbkge', weights.astype(jnp.bfloat16), key_pack[:,...  21.1 us
    reduce_sum x1, other arithmetic, shards(): attn_proj = jnp.sum(terms, axis=0)  18.9 us
    all_gather x1, waiting for transfers between devices, shards(): page_store = lax.all_gather(shared_pages, 'seq', axis=0, tiled=True)  16.8 us
    dot_general x4, matrix products, attend(): jnp.einsum('nbkge,bket->nbkgt', queries, key_pack[:, :, 0], preferred_ele...  14.5 us
    reduce_sum x3, other arithmetic, attend(): totals = jnp.sum(weights, -1)  13.6 us
  transfers between devices with their start and end apart: 4, of which 4 were waited for; matrix products, arithmetic and copies ran while one was open for 11% of the time, Pallas kernels for 0%

profile of v1, /device:TPU:1, one launch (start us, length us, event | category | flops | bytes accessed | tf_op | source)
XLA Modules:
  0.0 585.1 jit_solution(18383533720909590489)
XLA Ops:
  8.8 0.8 copy.88
  10.3 0.8 gather_fusion.9
  13.6 3.6 gather_fusion.11
  17.2 5.5 select_select_fusion
  22.7 8.8 %all-to-all-start = ((bf16[16,8,1,2,80,128]{5,4,3,1,2,0:T(8,128)(2,1)}), bf16[16,8,1,2,80,128]{5,4,3,1,2,0:T(8,128)(2,1)}, u32[]{:S(2)}, u32[]{:S(2)}) async-start(bf16[16,8,1,2,80,128]{5,4,3,1,2,0:T(8,128)(2,1)} %select_select_fusion), calls=%async_computation | async-start | bytes 10485760 | tf_op jit(solution)/shard_map/all_to_all | solution.py:160
  37.5 3.4 fusion.17
  40.9 3.0 fusion.19
  44.0 5.8 reshape.793
  49.7 2.6 convolution_convert_fusion
  55.5 2.8 fusion.73
  58.3 1.5 fusion.135
  60.3 1.1 fusion.30
  64.7 1.4 fusion.37
  66.4 5.5 fusion.26
  71.9 55.7 %all-to-all-done = bf16[16,8,1,2,80,128]{5,4,3,1,2,0:T(8,128)(2,1)} async-done(((bf16[16,8,1,2,80,128]{5,4,3,1,2,0:T(8,128)(2,1)}), bf16[16,8,1,2,80,128]{5,4,3,1,2,0:T(8,128)(2,1)}, u32[]{:S(2)}, u32[]{:S(2)}) %all-to-all-start) | async-done | bytes 5242912 | tf_op jit(solution)/shard_map/all_to_all | solution.py:160
  127.6 3.4 gather_fusion.12
  131.0 0.8 fusion.41
  132.3 1.5 reshape.788
  133.8 2.5 fusion.14
  136.3 3.2 copy-done.11
  139.7 2.7 fusion.15
  142.3 16.8 %all-gather.4.cloned.1.call-done = bf16[320,1,2,80,128]{4,3,2,1,0:T(8,128)(2,1)} async-done(((bf16[20,1,2,80,128]{4,3,2,1,0:T(8,128)(2,1)}), bf16[320,1,2,80,128]{4,3,2,1,0:T(8,128)(2,1)}) %all-gather.4.cloned.1.call-update) | async-done | bytes 13107216 | tf_op jit(solution)/shard_map/all_gather | solution.py:116
  159.2 7.1 %gather_fusion.15 = bf16[64,2,80,128]{3,2,1,0:T(8,128)(2,1)} fusion(bf16[320,2,80,128]{3,2,1,0:T(8,128)(2,1)} %bitcast.328, s32[1024]{0:T(1024)S(1)} %copy-done.31), kind=kCustom, calls=%fused_computation.1.clone | custom fusion | bytes 5243136 | tf_op jit(solution)/shard_map/jit(_take)/gather | solution.py:175
  166.2 7.2 %gather_fusion.14 = bf16[64,2,80,128]{3,2,1,0:T(8,128)(2,1)} fusion(bf16[320,2,80,128]{3,2,1,0:T(8,128)(2,1)} %bitcast.329, s32[1024]{0:T(1024)S(1)} %copy-done.30), kind=kCustom, calls=%fused_computation.clone | custom fusion | bytes 5243136 | tf_op jit(solution)/shard_map/jit(_take)/gather | solution.py:166
  173.4 4.2 fusion.35
  177.6 5.2 reshape.777
  182.8 4.3 fusion.34
  187.1 5.2 reshape.781
  192.3 8.8 %fusion.1 = (f32[128,4,4]{0,2,1:T(4,128)S(1)}, f32[4,2048,128,4]{2,1,3,0:T(8,128)}) fusion(pred[128,4,2048]{0,2,1:T(8,128)(4,1)S(1)} %copy-done.13, bf16[128,4,4,40]{0,3,2,1:T(8,128)(2,1)S(1)} %copy-done.24, bf16[128,4,4,40]{0,3,2,1:T(8,128)(2,1)S(1)} %copy-done.22, bf16[4,1,2,80,2048]{4,3,0,2,1:T(8,128)(2,1)} %reshape.781), kind=kOutput, calls=%fused_computation.21 | convolution fusion | flops 684324864 | bytes 19472384 | tf_op jit(solution)/shard_map/nbkge,bket->nbkgt/dot_general | solution.py:43
  201.1 2.7 fusion
  203.9 10.7 %fusion.2 = (f32[128,4,4]{0,2,1:T(4,128)S(1)}, f32[128,4,4]{0,2,1:T(4,128)S(1)}) fusion(f32[4,2048,128,4]{2,1,3,0:T(8,128)S(1)} %get-tuple-element.38, f32[128,4,4]{0,2,1:T(4,128)S(1)} %get-tuple-element.37, pred[128,4,2048]{0,2,1:T(8,128)(4,1)S(1)} %copy-done.12, f32[128,4,4]{0,2,1:T(4,128)S(1)} %get-tuple-element.31, ...), kind=kLoop, calls=%fused_computation.22 | loop fusion | flops 41938944 | bytes 35684352 | tf_op jit(solution)/shard_map/reduce_sum | solution.py:51
  214.7 3.0 fusion.56
  217.7 10.7 %fusion.68 = f32[128,4,1,4,80]{0,4,3,1,2:T(8,128)} fusion(f32[4,2048,128,4]{2,1,3,0:T(8,128)} %get-tuple-element.32, f32[128,4,4]{0,2,1:T(4,128)S(1)} %get-tuple-element.31, pred[128,4,2048]{0,2,1:T(8,128)(4,1)S(1)} %copy-done.13, bf16[4,1,2,80,2048]{4,3,0,2,1:T(8,128)(2,1)} %reshape.781, f32[128,4,4]{0,2,1:T(4,128)S(1)} %bitcast.344), kind=kOutput, calls=%fused_computation.94 | convolution fusion | flops 692224000 | bytes 19808256 | tf_op jit(solution)/shard_map/nbkgt,bket->nbkge/dot_general | solution.py:52
  228.4 5.8 fusion.65
  234.2 1.7 fusion.72
  236.7 3.9 fusion.123
  241.3 193.2 %all-gather.6.cloned.1.call-done = f32[4096,2560]{1,0:T(8,128)} async-done(((f32[512,2560]{1,0:T(8,128)}), f32[4096,2560]{1,0:T(8,128)}) %all-gather.6.cloned.1.call-update) | async-done | bytes 41943056 | tf_op jit(solution)/shard_map/all_gather | solution.py:191
  434.5 18.9 %reduce_sum.68 = f32[512,2560]{1,0:T(8,128)} reduce(f32[8,512,2560]{2,1,0:T(8,128)} %bitcast.321, f32[]{:T(128)} %constant.58.clone.1), dimensions={0}, to_apply=%region_11.13 | reduce | flops 9175040 | bytes 47185924 | tf_op jit(solution)/shard_map/reduce_sum | solution.py:192
  453.4 7.1 %reshape.798 = f32[128,4,2560]{2,1,0:T(4,128)} reshape(f32[512,2560]{1,0:T(8,128)} %reduce_sum.68) | data formatting | bytes 10485760 | tf_op jit(solution)/shard_map/reshape | solution.py:193
  460.5 5.1 multiply_reduce_fusion
  465.7 2.3 copy-done.9
  467.9 2.7 multiply_convert_fusion
  470.7 5.3 reshape.799
  476.0 5.5 fusion.124
  481.6 12.0 %fusion.78 = f32[512,2560]{1,0:T(8,128)} fusion(bf16[864,2560]{1,0:T(8,128)(2,1)} %param.32, f32[512,864]{0,1:T(8,128)S(1)} %fusion.124, bf16[512,2560]{1,0:T(8,128)(2,1)} %reshape.799, bf16[2560,864]{0,1:T(8,128)(2,1)} %param.31), kind=kOutput, calls=%fused_computation.102 | convolution fusion | flops 4532502528 | bytes 18481152 | tf_op jit(solution)/shard_map/dot_general | solution.py:202
  493.6 7.1 %reshape.800 = f32[128,4,2560]{2,1,0:T(4,128)} reshape(f32[512,2560]{1,0:T(8,128)} %fusion.78) | data formatting | bytes 10485760 | tf_op jit(solution)/shard_map/reshape | solution.py:204
  502.6 73.4 %all-reduce.3.cloned.1.call-done = f32[128,4,2560]{2,1,0:T(4,128)} async-done(((f32[128,4,2560]{2,1,0:T(4,128)}), f32[128,4,2560]{2,1,0:T(4,128)}) %all-reduce.3.cloned.1.call-update) | async-done | bytes 5242896
  576.0 2.3 dynamic-slice_add_fusion
  (164 shorter events, 21.9 us)
Async XLA Ops:
  6.5 230.2 %copy-start = (bf16[320,2560]{1,0:T(8,128)(2,1)S(1)}, bf16[320,2560]{1,0:T(8,128)(2,1)}, u32[]{:S(2)}) copy-start(bf16[320,2560]{1,0:T(8,128)(2,1)} %param.28) | copy-start | bytes 4915204
  6.5 152.6 %all-gather.4.cloned.1.call-start = ((), (), s32[]{:S(2)}) async-start(), calls=%async_computation.1 | async-start | bytes 13926400 | tf_op jit(solution)/shard_map/all_gather | solution.py:116
  10.3 3.3 copy-start.10
  22.7 9.0 %copy-start.1 = (s32[64]{0:T(128)S(1)}, s32[64]{0:T(128)}, u32[]{:S(2)}) copy-start(s32[64]{0:T(128)} %param.43) | copy-start | bytes 772
  22.7 10.3 %copy-start.2 = (s32[64]{0:T(128)S(1)}, s32[64]{0:T(128)}, u32[]{:S(2)}) copy-start(s32[64]{0:T(128)} %param.40) | copy-start | bytes 772
  22.7 10.9 %copy-start.3 = (s32[64]{0:T(128)S(1)}, s32[64]{0:T(128)}, u32[]{:S(2)}) copy-start(s32[64]{0:T(128)} %param.42) | copy-start | bytes 772
  22.7 11.6 %copy-start.4 = (s32[16]{0:T(128)S(1)}, s32[16]{0:T(128)}, u32[]{:S(2)}) copy-start(s32[16]{0:T(128)} %param.39) | copy-start | bytes 196
  22.7 12.2 %copy-start.5 = (s32[16]{0:T(128)S(1)}, s32[16]{0:T(128)}, u32[]{:S(2)}) copy-start(s32[16]{0:T(128)} %param.41) | copy-start | bytes 196
  22.7 12.9 %copy-start.26 = (s32[16,16]{1,0:T(8,128)S(1)}, s32[16,16]{1,0:T(8,128)}, u32[]{:S(2)}) copy-start(s32[16,16]{1,0:T(8,128)} %param.36) | copy-start | bytes 3076
  22.7 13.5 %copy-start.6 = (s32[4]{0:T(128)S(1)}, s32[4]{0:T(128)}, u32[]{:S(2)}) copy-start(s32[4]{0:T(128)} %param.38) | copy-start | bytes 52
  22.7 14.2 %copy-start.25 = (s32[4,16]{1,0:T(4,128)S(1)}, s32[4,16]{1,0:T(4,128)}, u32[]{:S(2)}) copy-start(s32[4,16]{1,0:T(4,128)} %param.35) | copy-start | bytes 772
  22.7 14.8 %copy-start.32 = (bf16[2560]{0:T(1024)(128)(2,1)S(1)}, bf16[2560]{0:T(1024)(128)(2,1)}, u32[]{:S(2)}) copy-start(bf16[2560]{0:T(1024)(128)(2,1)} %param.24) | copy-start | bytes 15364
  22.7 104.8 %all-to-all-start = ((bf16[16,8,1,2,80,128]{5,4,3,1,2,0:T(8,128)(2,1)}), bf16[16,8,1,2,80,128]{5,4,3,1,2,0:T(8,128)(2,1)}, u32[]{:S(2)}, u32[]{:S(2)}) async-start(bf16[16,8,1,2,80,128]{5,4,3,1,2,0:T(8,128)(2,1)} %select_select_fusion), calls=%async_computation | async-start | bytes 10485760 | tf_op jit(solution)/shard_map/all_to_all | solution.py:160
  31.6 402.9 %all-gather.6.cloned.1.call-start = ((), (), s32[]{:S(2)}) async-start(), calls=%async_computation.2 | async-start | bytes 47185920 | tf_op jit(solution)/shard_map/all_gather | solution.py:191
  37.5 3.4 copy-start.7
  40.9 8.8 %copy-start.20 = (bf16[2560,80]{0,1:T(8,128)(2,1)S(1)}, bf16[2560,80]{0,1:T(8,128)(2,1)}, u32[]{:S(2)}) copy-start(bf16[2560,80]{0,1:T(8,128)(2,1)} %param.27) | copy-start | bytes 1228804
  44.0 11.5 %copy-start.37 = (bf16[2560,80]{0,1:T(8,128)(2,1)S(1)}, bf16[2560,80]{0,1:T(8,128)(2,1)}, u32[]{:S(2)}) copy-start(bf16[2560,80]{0,1:T(8,128)(2,1)} %param.26) | copy-start | bytes 1228804
  53.1 5.2 copy-start.8
  55.5 4.9 copy-start.36
  61.5 0.7 copy-start.21
  61.6 1.0 copy-start.23
  62.6 2.1 copy-start.18
  66.2 70.2 %copy-start.15 = (pred[128,4,1024]{0,2,1:T(8,128)(4,1)}, pred[128,4,1024]{0,2,1:T(8,128)(4,1)S(1)}, u32[]{:S(2)}) copy-start(pred[128,4,1024]{0,2,1:T(8,128)(4,1)S(1)} %fusion.37) | copy-start | bytes 1572868
  136.3 3.2 copy-start.11
  136.3 3.3 copy-start.27
  139.7 19.5 %copy-start.31 = (s32[1024]{0:T(1024)S(1)}, s32[1024]{0:T(1024)}, u32[]{:S(2)}) copy-start(s32[1024]{0:T(1024)} %pad_clamp_fusion.4) | copy-start | bytes 12292
  142.3 23.9 %copy-start.30 = (s32[1024]{0:T(1024)S(1)}, s32[1024]{0:T(1024)}, u32[]{:S(2)}) copy-start(s32[1024]{0:T(1024)} %pad_clamp_fusion.5) | copy-start | bytes 12292
  159.2 14.3 %copy-start.35 = (pred[4,16]{1,0:T(4,128)(4,1)S(1)}, pred[4,16]{1,0:T(4,128)(4,1)}, u32[]{:S(2)}) copy-start(pred[4,16]{1,0:T(4,128)(4,1)} %compare_and_fusion.2) | copy-start | bytes 196
  173.4 9.4 %copy-start.34 = (pred[4,16]{1,0:T(4,128)(4,1)S(1)}, pred[4,16]{1,0:T(4,128)(4,1)}, u32[]{:S(2)}) copy-start(pred[4,16]{1,0:T(4,128)(4,1)} %compare_and_fusion.1) | copy-start | bytes 196
  182.8 9.5 %copy-start.13 = (pred[128,4,2048]{0,2,1:T(8,128)(4,1)S(1)}, pred[128,4,2048]{0,2,1:T(8,128)(4,1)}, u32[]{:S(2)}) copy-start(pred[128,4,2048]{0,2,1:T(8,128)(4,1)} %get-tuple-element.28) | copy-start | bytes 3145732
  182.8 9.5 %copy-start.22 = (bf16[128,4,4,40]{0,3,2,1:T(8,128)(2,1)S(1)}, bf16[128,4,4,40]{0,3,2,1:T(8,128)(2,1)}, u32[]{:S(2)}) copy-start(bf16[128,4,4,40]{0,3,2,1:T(8,128)(2,1)} %copy-done.21) | copy-start | bytes 491524
  182.8 9.5 %copy-start.24 = (bf16[128,4,4,40]{0,3,2,1:T(8,128)(2,1)S(1)}, bf16[128,4,4,40]{0,3,2,1:T(8,128)(2,1)}, u32[]{:S(2)}) copy-start(bf16[128,4,4,40]{0,3,2,1:T(8,128)(2,1)} %copy-done.23) | copy-start | bytes 491524
  192.3 8.8 %copy-start.12 = (pred[128,4,2048]{0,2,1:T(8,128)(4,1)S(1)}, pred[128,4,2048]{0,2,1:T(8,128)(4,1)}, u32[]{:S(2)}) copy-start(pred[128,4,2048]{0,2,1:T(8,128)(4,1)} %get-tuple-element.27) | copy-start | bytes 3145732
  192.3 8.8 %copy-start.14 = (bf16[4,1,2,80,2048]{4,3,0,2,1:T(8,128)(2,1)S(1)}, bf16[4,1,2,80,2048]{4,3,0,2,1:T(8,128)(2,1)}, u32[]{:S(2)}) copy-start(bf16[4,1,2,80,2048]{4,3,0,2,1:T(8,128)(2,1)} %reshape.777) | copy-start | bytes 7864324
  201.1 13.6 %slice-start = ((s8[8388608]{0:T(1024)(128)(4,1)}), s8[4194304]{0:T(1024)(128)(4,1)S(1)}, s32[]{:S(2)}) async-start(s8[8388608]{0:T(1024)(128)(4,1)} %bitcast.326), calls=%async_computation.4 | async-start | bytes 8388608
  203.9 10.8 %copy-start.28 = (f32[128,4,4]{0,2,1:T(4,128)S(1)}, f32[128,4,4]{0,2,1:T(4,128)}, u32[]{:S(2)}) copy-start(f32[128,4,4]{0,2,1:T(4,128)} %copy-done.27) | copy-start | bytes 24580
  203.9 10.8 %copy-start.29 = (f32[128,4,4]{0,2,1:T(4,128)S(1)}, f32[128,4,4]{0,2,1:T(4,128)}, u32[]{:S(2)}) copy-start(f32[128,4,4]{0,2,1:T(4,128)} %fusion.15) | copy-start | bytes 24580
  203.9 10.8 %slice-start.1 = ((s8[8388608]{0:T(1024)(128)(4,1)}), s8[4194304]{0:T(1024)(128)(4,1)S(1)}, s32[]{:S(2)}) async-start(s8[8388608]{0:T(1024)(128)(4,1)} %bitcast.326), calls=%async_computation.5 | async-start | bytes 8388608
  203.9 10.8 %copy-start.16 = (pred[128,4,1024]{0,2,1:T(8,128)(4,1)S(1)}, pred[128,4,1024]{0,2,1:T(8,128)(4,1)}, u32[]{:S(2)}) copy-start(pred[128,4,1024]{0,2,1:T(8,128)(4,1)} %copy-done.15) | copy-start | bytes 1572868
  203.9 10.8 %copy-start.17 = (bf16[4,1,2,80,1024]{4,3,0,2,1:T(8,128)(2,1)S(1)}, bf16[4,1,2,80,1024]{4,3,0,2,1:T(8,128)(2,1)}, u32[]{:S(2)}) copy-start(bf16[4,1,2,80,1024]{4,3,0,2,1:T(8,128)(2,1)} %reshape.788) | copy-start | bytes 3932164
  228.4 5.8 copy-start.19
  240.6 0.7 copy-start.33
  240.6 335.4 %all-reduce.3.cloned.1.call-start = ((), (), s32[]{:S(2)}) async-start(), calls=%async_computation.3 | async-start | bytes 10485760
  465.6 2.3 copy-start.9
  500.7 0.7 copy-start.38
Sparse Core Ops, SparseCore 0:
  9.5 149.6 all-gather.3
  240.8 193.7 all-gather.5
  500.9 75.0 all-reduce.2
